TPU v7x, 512 devices: a whole 4x4x16 slice. The times are simulated.
512 devices in a mesh: req: 8 (over z_lo), row: 8 (over x, core), col: 8 (over y, z_hi).
Axes of the slice: x: 4, y: 4, z: 16 (z_hi: 2, z_lo: 8; z = z_hi * 8 + z_lo), core: 2. Of those that a mesh axis runs over, the one named last changes fastest.
Arguments:
- tokens: bfloat16 [1792, 32768], P('col', ('req', 'row')), may hold values from -6 to 6
- qkv_weight: bfloat16 [1792, 2304], P('col', 'row'), may hold values from -0.125 to 0.125
- out_weight: bfloat16 [1792, 1792], P('row', 'col'), may hold values from -0.125 to 0.125
- head_gain: float32 [1792], P('row'), may hold values from 0.1 to 1.9
- prefix_keys: bfloat16 [24, 256, 8192], P('req', 'row', 'col'), may hold values from -6 to 6
- prefix_values: bfloat16 [24, 1792, 8192], P('req', 'row', 'col'), may hold values from -6 to 6
- suffix_len: int32 [64], P(('req', 'col')), may hold values from 1 to 512, 24576 in all
- prefix_owner: int32 [64], P(('req', 'col')), may hold values from 0 to 23
Outputs:
- layer_out: bfloat16 [1792, 32768], P('col', ('req', 'row'))
Inputs may be any that keep to these rules, and one draw needn't show every extreme that they name: `suffix_len`: the longest suffix has exactly 512 live tokens.
All inputs are finite; a program needn't handle non-finite values. No bound on the sum of `suffix_len` on one device may be relied on, other than what follows from the above.
Results may differ from a plain program's by a relative error of at most 0.015.
Values may be sent and summed in bfloat16 or wider, within the bound.
No kernel may reach another device: no remote copies, remote signals or barrier semaphores. Data moves between devices by JAX's collectives and lax.ppermute only.
A program may use at most 64 MiB of HBM per device.

v0:
```python
import jax
import jax.numpy as jnp
import numpy as np
from jax import lax
from jax.sharding import Mesh, PartitionSpec as P

FEAT = 16
SLOTS = 512
HD = 112
ROW = ("x", "c")
COL = ("y", "zh")
epsilon = 1e-05


def feature_map(values_in):
    feature_count = values_in.shape[-1]
    squares = (values_in[..., :, None] * values_in[..., None, :]).reshape(
        values_in.shape[:-1] + (feature_count * feature_count,)
    )
    constant = jnp.ones(values_in.shape[:-1] + (1,), jnp.float32)
    linear = values_in * feature_count ** (-0.25)
    quadratic = squares * (0.5**0.5 / feature_count**0.5)
    return jnp.concatenate([constant, linear, quadratic], axis=-1).astype(jnp.bfloat16)


def feature_columns(values_in):
    feature_count = values_in.shape[-2]
    length = values_in.shape[-1]
    squares = (values_in[..., :, None, :] * values_in[..., None, :, :]).reshape(
        values_in.shape[:-2] + (feature_count * feature_count, length)
    )
    constant = jnp.ones(values_in.shape[:-2] + (1, length), jnp.float32)
    linear = values_in * feature_count ** (-0.25)
    quadratic = squares * (0.5**0.5 / feature_count**0.5)
    return jnp.concatenate([constant, linear, quadratic], axis=-2).astype(jnp.bfloat16)


def shards(
    tokens, qkv_weight, out_weight, head_gain, prefix_keys, prefix_values, suffix_len, prefix_owner
):
    n_col = lax.psum(1, COL)
    heads_here = head_gain.shape[0] // HD
    partial_proj = lax.dot_general(
        lax.all_gather(tokens, ROW, axis=1, tiled=True),
        qkv_weight,
        (((0,), (0,)), ((), ())),
        preferred_element_type=jnp.float32,
    ).astype(jnp.bfloat16)
    projected = lax.psum_scatter(partial_proj, "y", scatter_dimension=0, tiled=True)
    projected = lax.psum_scatter(projected, "zh", scatter_dimension=0, tiled=True)
    projected = projected.reshape(SLOTS, heads_here, 2 * FEAT + HD)
    queries = projected[..., :FEAT]
    keys_now = projected[..., FEAT : 2 * FEAT]
    values_now = projected[..., 2 * FEAT :]
    pref_here = prefix_keys.shape[0]
    plen_here = prefix_keys.shape[2]
    feats_cached = feature_columns(
        prefix_keys.reshape(pref_here, heads_here, FEAT, plen_here).astype(jnp.float32)
    )
    values_cached = prefix_values.reshape(pref_here, heads_here, HD, plen_here)
    partial_state = jnp.einsum(
        "phet,phvt->phev", feats_cached, values_cached, preferred_element_type=jnp.float32
    )
    state_shape = partial_state.shape[1:]
    piece = partial_state[0].size // n_col
    pieces = partial_state.astype(jnp.bfloat16).reshape(pref_here, n_col, piece)
    pieces = jnp.swapaxes(pieces, 0, 1)
    pieces = lax.psum_scatter(pieces, "y", scatter_dimension=0, tiled=True)
    pieces = lax.psum_scatter(pieces, "zh", scatter_dimension=0, tiled=True)
    pieces = lax.all_gather(pieces[0], "req", axis=0, tiled=True)
    owners = lax.all_gather(prefix_owner, COL, axis=0, tiled=True)
    to_send = jnp.take(pieces, owners, axis=0)
    chosen = lax.all_to_all(to_send, COL, 0, 0, tiled=True)
    chosen = chosen.reshape(state_shape).astype(jnp.float32)
    feats_query = feature_map(queries.astype(jnp.float32)).astype(jnp.float32)
    carried = jnp.einsum("the,hev->thv", feats_query, chosen, precision=lax.Precision.HIGHEST)
    scores = jnp.einsum("thf,shf->hts", queries, keys_now, preferred_element_type=jnp.float32)
    weights = 1.0 + scores * FEAT ** (-0.5) + scores * scores * (0.5 / FEAT)
    positions = jnp.arange(SLOTS, dtype=jnp.int32)
    length = suffix_len[0]
    allowed = (positions[None, :] <= positions[:, None]) & (positions[None, :] < length)
    weights = jnp.where(allowed[None], weights, 0.0).astype(jnp.bfloat16)
    within = jnp.einsum("hts,shv->thv", weights, values_now, preferred_element_type=jnp.float32)
    active = (positions < length)[:, None, None]
    attended = jnp.where(active, carried + within, 0.0)
    inverse_rms = lax.rsqrt(jnp.mean(attended * attended, axis=-1, keepdims=True) + epsilon)
    gains = head_gain.reshape(heads_here, HD)
    normed = (attended * inverse_rms * gains).astype(jnp.bfloat16).reshape(SLOTS, heads_here * HD)
    gathered = lax.all_gather(normed, "zh", axis=0, tiled=True)
    gathered = lax.all_gather(gathered, "y", axis=0, tiled=True)
    out_terms = lax.dot_general(
        out_weight, gathered, (((0,), (1,)), ((), ())), preferred_element_type=jnp.float32
    )
    mixed_sums = lax.psum_scatter(
        out_terms.astype(jnp.bfloat16), ROW, scatter_dimension=1, tiled=True
    ).astype(jnp.float32)
    return (tokens.astype(jnp.float32) + mixed_sums).astype(jnp.bfloat16)


def solution(mesh):
    n_req, n_row, n_col = (mesh.shape[a] for a in ("req", "row", "col"))
    fine = Mesh(
        np.asarray(mesh.devices).reshape(n_req, n_row // 2, 2, n_col // 2, 2),
        ("req", "x", "c", "y", "zh"),
    )
    in_specs = (
        P(COL, ("req",) + ROW),
        P(COL, ROW),
        P(ROW, COL),
        P(ROW),
        P("req", ROW, COL),
        P("req", ROW, COL),
        P(("req",) + COL),
        P(("req",) + COL),
    )
    out_specs = P(COL, ("req",) + ROW)
    return jax.shard_map(shards, mesh=fine, in_specs=in_specs, out_specs=out_specs, check_vma=False)
```

profile of v0, /device:TPU:8, one launch (start us, length us, event | category | flops | bytes accessed | tf_op | source)
XLA Modules:
  0.0 352.4 jit_solution(18403591849002129596)
XLA Ops:
  7.4 1.1 convert.23
  8.4 1.0 multiply_convert_fusion.3
  10.3 1.3 fusion.8
  11.7 0.9 reshape.122
  12.6 1.1 copy.14
  14.3 1.3 dynamic-slice.1
  16.2 59.5 %all-reduce.6.cloned.1.call-done = bf16[8,3,7644]{2,1,0:T(4,128)(2,1)} async-done(((bf16[8,3,7644]{2,1,0:T(4,128)(2,1)}), bf16[8,3,7644]{2,1,0:T(4,128)(2,1)}) %all-reduce.6.cloned.1.call-update) | async-done | bytes 366928
  75.8 1.6 constant_dynamic-slice_fusion.1
  77.5 3.7 %convolution_convert_fusion = bf16[4096,288]{0,1:T(8,128)(2,1)} fusion(bf16[224,288]{0,1:T(8,128)(2,1)S(1)} %copy-done.2, bf16[224,4096]{1,0:T(8,128)(2,1)} %all-gather.4.cloned.1.call-done), kind=kOutput, calls=%fused_computation.2 | convolution fusion | flops 529661952 | bytes 4323328 | tf_op jit(solution)/shard_map/dot_general | solution.py:43
  81.9 1.3 dynamic-slice
  83.9 19.5 %all-reduce = s32[8]{0:T(128)S(1)} all-reduce(s32[8]{0:T(128)S(1)} %dynamic-update-slice), channel_id=1, replica_groups=mesh['req'=8,'x'=4,'c'=2,'y'=4,'zh'=2] {'y','zh'}, use_global_device_ids=true, to_apply=%add | all-reduce | flops 8 | bytes 64
  103.4 1.3 dynamic-slice.3
  104.7 34.3 %all-reduce.8.cloned.1.call-done = bf16[2,3,7644]{2,1,0:T(4,128)(2,1)} async-done(((bf16[2,3,7644]{2,1,0:T(4,128)(2,1)}), bf16[2,3,7644]{2,1,0:T(4,128)(2,1)}) %all-reduce.8.cloned.1.call-update) | async-done | bytes 91744
  139.0 1.5 constant_dynamic-slice_fusion
  140.6 48.8 %all-gather = bf16[1,24,7644]{2,0,1:T(2,128)(2,1)S(1)} all-gather(bf16[1,3,7644]{2,0,1:T(2,128)(2,1)S(1)} %copy.15), channel_id=2, replica_groups=mesh['req'=8,'x'=4,'c'=2,'y'=4,'zh'=2] {'req'}, dimensions={1}, use_global_device_ids=true | all-gather | bytes 412776 | tf_op jit(solution)/shard_map/all_gather | solution.py:70
  192.3 4.8 %all-to-all-start = ((bf16[8,2,3822]{2,1,0:T(2,128)(2,1)}), bf16[8,2,3822]{2,1,0:T(2,128)(2,1)S(1)}, u32[]{:S(2)}, u32[]{:S(2)}) async-start(bf16[8,2,3822]{2,1,0:T(2,128)(2,1)} %reshape.147), calls=%async_computation | async-start | bytes 245760 | tf_op jit(solution)/shard_map/all_to_all | solution.py:73
  197.9 13.7 %all-to-all-done = bf16[8,2,3822]{2,1,0:T(2,128)(2,1)S(1)} async-done(((bf16[8,2,3822]{2,1,0:T(2,128)(2,1)}), bf16[8,2,3822]{2,1,0:T(2,128)(2,1)S(1)}, u32[]{:S(2)}, u32[]{:S(2)}) %all-to-all-start) | async-done | bytes 122336 | tf_op jit(solution)/shard_map/all_to_all | solution.py:73
  212.8 23.3 %reduce-scatter.6.cloned.1.call-done = bf16[512,288]{0,1:T(8,128)(2,1)} async-done(((bf16[1024,288]{0,1:T(8,128)(2,1)}), bf16[512,288]{0,1:T(8,128)(2,1)}) %reduce-scatter.6.cloned.1.call-update) | async-done | bytes 294928 | tf_op jit(solution)/shard_map/reduce_scatter | solution.py:50
  237.6 1.9 fusion.7
  240.2 28.6 %all_gather.18 = bf16[1024,224]{0,1:T(8,128)(2,1)} all-gather(bf16[512,224]{0,1:T(8,128)(2,1)S(1)} %bitcast.34), channel_id=1, replica_groups=mesh['req'=8,'x'=4,'c'=2,'y'=4,'zh'=2] {'zh'}, dimensions={0}, use_global_device_ids=true | all-gather | bytes 688128 | tf_op jit(solution)/shard_map/all_gather | solution.py:89
  269.0 29.1 %all-gather.6.cloned.1.call-done = bf16[4096,224]{0,1:T(8,128)(2,1)} async-done(((bf16[1024,224]{0,1:T(8,128)(2,1)}), bf16[4096,224]{0,1:T(8,128)(2,1)}) %all-gather.6.cloned.1.call-update) | async-done | bytes 1835024 | tf_op jit(solution)/shard_map/all_gather | solution.py:90
  298.1 3.4 fusion
  301.5 42.1 %reduce-scatter.8.cloned.1.call-done = bf16[224,512]{1,0:T(8,128)(2,1)} async-done(((bf16[224,4096]{1,0:T(8,128)(2,1)}), bf16[224,512]{1,0:T(8,128)(2,1)}) %reduce-scatter.8.cloned.1.call-update) | async-done | bytes 229392 | tf_op jit(solution)/shard_map/reduce_scatter | solution.py:94
  343.6 1.7 add_convert_fusion
  (52 shorter events, 9.0 us)
Async XLA Ops:
  7.4 3.0 copy-start
  7.4 68.4 %all-reduce.6.cloned.1.call-start = ((), (), s32[]{:S(2)}) async-start(), calls=%async_computation.9 | async-start | bytes 983040
  11.6 65.8 %copy-start.2 = (bf16[224,288]{0,1:T(8,128)(2,1)S(1)}, bf16[224,288]{0,1:T(8,128)(2,1)}, u32[]{:S(2)}) copy-start(bf16[224,288]{0,1:T(8,128)(2,1)} %param.9) | copy-start | bytes 387076
  13.7 63.8 %all-gather.4.cloned.1.call-start = ((), (), s32[]{:S(2)}) async-start(), calls=%async_computation.4 | async-start | bytes 2064384 | tf_op jit(solution)/shard_map/all_gather | solution.py:44
  14.2 124.8 %all-reduce.8.cloned.1.call-start = ((), (), s32[]{:S(2)}) async-start(), calls=%async_computation.10 | async-start | bytes 245760
  77.4 112.7 %reduce-scatter.4.cloned.1.call-start = ((), (), s32[]{:S(2)}) async-start(), calls=%async_computation.5 | async-start | bytes 2949120 | tf_op jit(solution)/shard_map/reduce_scatter | solution.py:49
  81.2 154.9 %reduce-scatter.6.cloned.1.call-start = ((), (), s32[]{:S(2)}) async-start(), calls=%async_computation.6 | async-start | bytes 884736 | tf_op jit(solution)/shard_map/reduce_scatter | solution.py:50
  189.4 8.3 %copy-start.4 = (f32[224]{0:T(256)S(1)}, f32[224]{0:T(256)}, u32[]{:S(2)}) copy-start(f32[224]{0:T(256)} %param.11) | copy-start | bytes 2692
  192.3 19.3 %all-to-all-start = ((bf16[8,2,3822]{2,1,0:T(2,128)(2,1)}), bf16[8,2,3822]{2,1,0:T(2,128)(2,1)S(1)}, u32[]{:S(2)}, u32[]{:S(2)}) async-start(bf16[8,2,3822]{2,1,0:T(2,128)(2,1)} %reshape.147), calls=%async_computation | async-start | bytes 245760 | tf_op jit(solution)/shard_map/all_to_all | solution.py:73
  197.1 101.0 %all-gather.6.cloned.1.call-start = ((), (), s32[]{:S(2)}) async-start(), calls=%async_computation.7 | async-start | bytes 2293760 | tf_op jit(solution)/shard_map/all_gather | solution.py:90
  239.5 58.6 %copy-start.3 = (bf16[224,224]{1,0:T(8,128)(2,1)S(1)}, bf16[224,224]{1,0:T(8,128)(2,1)}, u32[]{:S(2)}) copy-start(bf16[224,224]{1,0:T(8,128)(2,1)} %param.10) | copy-start | bytes 301060
  268.9 74.7 %copy-start.1 = (bf16[224,512]{1,0:T(8,128)(2,1)S(1)}, bf16[224,512]{1,0:T(8,128)(2,1)}, u32[]{:S(2)}) copy-start(bf16[224,512]{1,0:T(8,128)(2,1)} %param.8) | copy-start | bytes 688132
  268.9 74.7 %reduce-scatter.8.cloned.1.call-start = ((), (), s32[]{:S(2)}) async-start(), calls=%async_computation.8 | async-start | bytes 2064384 | tf_op jit(solution)/shard_map/reduce_scatter | solution.py:94
Sparse Core Ops, SparseCore 0:
  13.8 61.9 all-reduce.5
  78.6 60.3 all-reduce.7
  141.9 29.7 reduce-scatter.3
  190.3 45.7 reduce-scatter.5
  269.0 28.9 all-gather.5
Sparse Core Ops, SparseCore 1:
  16.3 36.7 all-gather.3
  301.6 42.0 reduce-scatter.7
where the time goes:
time: 353 us; the launch traced here: 352 us
  waiting for transfers between devices  203 us (58%)
  blocking collectives  97 us (27%)
  between operations  16.7 us (5%)
  local copies, waits for them, and re-layouts  12.2 us (3%)
  matrix products  10.8 us (3%)
  other arithmetic  7.93 us (2%)
  starting transfers between devices  5.03 us (1%)
    unnamed x9, waiting for transfers between devices  94.5 us
    all_gather x1, blocking collectives, shards(): pieces = lax.all_gather(pieces[0], 'req', axis=0, tiled=True)  48.8 us
    reduce_scatter x1, waiting for transfers between devices, shards(): lax.psum_scatter(out_terms.astype(jnp.bfloat16), ROW, scatter_dimension=1...  42.1 us
    all_gather x1, waiting for transfers between devices, shards(): gathered = lax.all_gather(gathered, 'y', axis=0, tiled=True)  29.1 us
    all_gather x1, blocking collectives, shards(): gathered = lax.all_gather(normed, 'zh', axis=0, tiled=True)  28.6 us
    reduce_scatter x1, waiting for transfers between devices, shards(): lax.psum_scatter(projected, 'zh', scatter_dimension=0, tiled=True)  23.3 us
    unnamed x1, blocking collectives  19.5 us
    all_to_all x1, waiting for transfers between devices, shards(): chosen = lax.all_to_all(to_send, COL, 0, 0, tiled=True)  13.7 us
  transfers between devices with their start and end apart: 8, of which 6 were waited for; matrix products, arithmetic and copies ran while one was open for 4% of the time, Pallas kernels for 0%

commit v1 on v0

--- a/solution.py
+++ b/solution.py
@@ -87,7 +87,9 @@
     gains = head_gain.reshape(heads_here, HD)
     normed = (attended * inverse_rms * gains).astype(jnp.bfloat16).reshape(SLOTS, heads_here * HD)
     gathered = lax.all_gather(normed, "zh", axis=0, tiled=True)
-    gathered = lax.all_gather(gathered, "y", axis=0, tiled=True)
+    gathered = jnp.concatenate(
+        lax.all_to_all(jnp.stack([gathered] * lax.axis_size("y")), "y", 0, 0), axis=0
+    )
     out_terms = lax.dot_general(
         out_weight, gathered, (((0,), (1,)), ((), ())), preferred_element_type=jnp.float32
     )

time: 353 us -> 341 us (0.966)
  the two profiles are of different devices: /device:TPU:8 before, /device:TPU:16 now
where the time goes in v1:
time: 341 us
  waiting for transfers between devices  168 us (49%)
  blocking collectives  120 us (35%)
  between operations  16.7 us (5%)
  local copies, waits for them, and re-layouts  13.2 us (4%)
  matrix products  9.36 us (3%)
  other arithmetic  7.93 us (2%)
  starting transfers between devices  4.98 us (1%)
    unnamed x8, waiting for transfers between devices  96 us
    all_gather x1, blocking collectives, shards(): pieces = lax.all_gather(pieces[0], 'req', axis=0, tiled=True)  48.9 us
    reduce_scatter x1, waiting for transfers between devices, shards(): lax.psum_scatter(out_terms.astype(jnp.bfloat16), ROW, scatter_dimension=1...  35.1 us
    all_gather x1, blocking collectives, shards(): gathered = lax.all_gather(normed, 'zh', axis=0, tiled=True)  28.5 us
    all_to_all x1, blocking collectives, shards(): lax.all_to_all(jnp.stack([gathered] * lax.axis_size('y')), 'y', 0, 0)  25 us
    reduce_scatter x1, waiting for transfers between devices, shards(): lax.psum_scatter(projected, 'zh', scatter_dimension=0, tiled=True)  23.6 us
    unnamed x1, blocking collectives  18 us
    all_to_all x1, waiting for transfers between devices, shards(): chosen = lax.all_to_all(to_send, COL, 0, 0, tiled=True)  13.4 us
  transfers between devices with their start and end apart: 7, of which 5 were waited for; matrix products, arithmetic and copies ran while one was open for 5% of the time, Pallas kernels for 0%

profile of v1, /device:TPU:16, one launch (start us, length us, event | category | flops | bytes accessed | tf_op | source)
XLA Modules:
  0.0 340.7 jit_solution(17626835292777369966)
XLA Ops:
  7.4 1.1 convert.23
  8.4 1.0 multiply_convert_fusion.3
  10.3 1.3 fusion.8
  11.7 0.9 reshape.127
  12.6 1.0 copy.16
  14.3 1.3 dynamic-slice.1
  16.2 59.7 %all-reduce.6.cloned.1.call-done = bf16[8,3,7644]{2,1,0:T(4,128)(2,1)} async-done(((bf16[8,3,7644]{2,1,0:T(4,128)(2,1)}), bf16[8,3,7644]{2,1,0:T(4,128)(2,1)}) %all-reduce.6.cloned.1.call-update) | async-done | bytes 366928
  75.9 1.6 constant_dynamic-slice_fusion.1
  77.6 3.7 %convolution_convert_fusion = bf16[4096,288]{0,1:T(8,128)(2,1)} fusion(bf16[224,288]{0,1:T(8,128)(2,1)S(1)} %copy-done.2, bf16[224,4096]{1,0:T(8,128)(2,1)} %all-gather.3.cloned.1.call-done), kind=kOutput, calls=%fused_computation.2 | convolution fusion | flops 529661952 | bytes 4323328 | tf_op jit(solution)/shard_map/dot_general | solution.py:43
  82.0 1.3 dynamic-slice
  83.9 18.0 %all-reduce = s32[8]{0:T(128)S(1)} all-reduce(s32[8]{0:T(128)S(1)} %dynamic-update-slice), channel_id=1, replica_groups=mesh['req'=8,'x'=4,'c'=2,'y'=4,'zh'=2] {'y','zh'}, use_global_device_ids=true, to_apply=%add | all-reduce | flops 8 | bytes 64
  101.9 1.3 dynamic-slice.3
  103.2 35.7 %all-reduce.8.cloned.1.call-done = bf16[2,3,7644]{2,1,0:T(4,128)(2,1)} async-done(((bf16[2,3,7644]{2,1,0:T(4,128)(2,1)}), bf16[2,3,7644]{2,1,0:T(4,128)(2,1)}) %all-reduce.8.cloned.1.call-update) | async-done | bytes 91744
  138.9 1.4 constant_dynamic-slice_fusion
  140.4 48.9 %all-gather = bf16[1,24,7644]{2,0,1:T(2,128)(2,1)S(1)} all-gather(bf16[1,3,7644]{2,0,1:T(2,128)(2,1)S(1)} %copy.17), channel_id=2, replica_groups=mesh['req'=8,'x'=4,'c'=2,'y'=4,'zh'=2] {'req'}, dimensions={1}, use_global_device_ids=true | all-gather | bytes 412776 | tf_op jit(solution)/shard_map/all_gather | solution.py:70
  192.1 4.8 %all-to-all-start = ((bf16[8,2,3822]{2,1,0:T(2,128)(2,1)}), bf16[8,2,3822]{2,1,0:T(2,128)(2,1)S(1)}, u32[]{:S(2)}, u32[]{:S(2)}) async-start(bf16[8,2,3822]{2,1,0:T(2,128)(2,1)} %reshape.153), calls=%async_computation | async-start | bytes 245760 | tf_op jit(solution)/shard_map/all_to_all | solution.py:73
  197.7 13.4 %all-to-all-done = bf16[8,2,3822]{2,1,0:T(2,128)(2,1)S(1)} async-done(((bf16[8,2,3822]{2,1,0:T(2,128)(2,1)}), bf16[8,2,3822]{2,1,0:T(2,128)(2,1)S(1)}, u32[]{:S(2)}, u32[]{:S(2)}) %all-to-all-start) | async-done | bytes 122336 | tf_op jit(solution)/shard_map/all_to_all | solution.py:73
  212.3 23.6 %reduce-scatter.6.cloned.1.call-done = bf16[512,288]{0,1:T(8,128)(2,1)} async-done(((bf16[1024,288]{0,1:T(8,128)(2,1)}), bf16[512,288]{0,1:T(8,128)(2,1)}) %reduce-scatter.6.cloned.1.call-update) | async-done | bytes 294928 | tf_op jit(solution)/shard_map/reduce_scatter | solution.py:50
  237.4 1.9 fusion.7
  240.1 28.5 %all_gather.15 = bf16[1024,224]{0,1:T(8,128)(2,1)S(1)} all-gather(bf16[512,224]{0,1:T(8,128)(2,1)S(1)} %bitcast.38), channel_id=1, replica_groups=mesh['req'=8,'x'=4,'c'=2,'y'=4,'zh'=2] {'zh'}, dimensions={0}, use_global_device_ids=true | all-gather | bytes 688128 | tf_op jit(solution)/shard_map/all_gather | solution.py:89
  268.8 25.0 %all_to_all.11 = bf16[4,1024,224]{1,2,0:T(8,128)(2,1)S(1)} all-to-all(bf16[4,1024,224]{1,2,0:T(8,128)(2,1)S(1)} %stack.2), channel_id=1, replica_groups=mesh['req'=8,'x'=4,'c'=2,'y'=4,'zh'=2] {'y'}, dimensions={0} | all-to-all | bytes 3670016 | tf_op jit(solution)/shard_map/all_to_all | solution.py:91
  294.7 2.0 fusion
  296.7 35.1 %reduce-scatter.8.cloned.1.call-done = bf16[224,512]{1,0:T(8,128)(2,1)} async-done(((bf16[224,4096]{1,0:T(8,128)(2,1)}), bf16[224,512]{1,0:T(8,128)(2,1)}) %reduce-scatter.8.cloned.1.call-update) | async-done | bytes 229392 | tf_op jit(solution)/shard_map/reduce_scatter | solution.py:96
  331.9 1.7 add_convert_fusion
  (52 shorter events, 10.0 us)
Async XLA Ops:
  7.4 3.0 copy-start
  7.4 68.5 %all-reduce.6.cloned.1.call-start = ((), (), s32[]{:S(2)}) async-start(), calls=%async_computation.9 | async-start | bytes 983040
  11.6 65.9 %copy-start.2 = (bf16[224,288]{0,1:T(8,128)(2,1)S(1)}, bf16[224,288]{0,1:T(8,128)(2,1)}, u32[]{:S(2)}) copy-start(bf16[224,288]{0,1:T(8,128)(2,1)} %param.9) | copy-start | bytes 387076
  13.6 63.9 %all-gather.3.cloned.1.call-start = ((), (), s32[]{:S(2)}) async-start(), calls=%async_computation.5 | async-start | bytes 2064384 | tf_op jit(solution)/shard_map/all_gather | solution.py:44
  14.2 124.7 %all-reduce.8.cloned.1.call-start = ((), (), s32[]{:S(2)}) async-start(), calls=%async_computation.10 | async-start | bytes 245760
  77.5 112.5 %reduce-scatter.4.cloned.1.call-start = ((), (), s32[]{:S(2)}) async-start(), calls=%async_computation.6 | async-start | bytes 2949120 | tf_op jit(solution)/shard_map/reduce_scatter | solution.py:49
  81.3 154.6 %reduce-scatter.6.cloned.1.call-start = ((), (), s32[]{:S(2)}) async-start(), calls=%async_computation.7 | async-start | bytes 884736 | tf_op jit(solution)/shard_map/reduce_scatter | solution.py:50
  189.3 8.3 %copy-start.4 = (f32[224]{0:T(256)S(1)}, f32[224]{0:T(256)}, u32[]{:S(2)}) copy-start(f32[224]{0:T(256)} %param.11) | copy-start | bytes 2692
  192.1 19.0 %all-to-all-start = ((bf16[8,2,3822]{2,1,0:T(2,128)(2,1)}), bf16[8,2,3822]{2,1,0:T(2,128)(2,1)S(1)}, u32[]{:S(2)}, u32[]{:S(2)}) async-start(bf16[8,2,3822]{2,1,0:T(2,128)(2,1)} %reshape.153), calls=%async_computation | async-start | bytes 245760 | tf_op jit(solution)/shard_map/all_to_all | solution.py:73
  196.9 134.9 %reduce-scatter.8.cloned.1.call-start = ((), (), s32[]{:S(2)}) async-start(), calls=%async_computation.8 | async-start | bytes 2064384 | tf_op jit(solution)/shard_map/reduce_scatter | solution.py:96
  293.8 0.9 copy-start.3
  294.7 37.1 %copy-start.1 = (bf16[224,512]{1,0:T(8,128)(2,1)S(1)}, bf16[224,512]{1,0:T(8,128)(2,1)}, u32[]{:S(2)}) copy-start(bf16[224,512]{1,0:T(8,128)(2,1)} %param.8) | copy-start | bytes 688132
Sparse Core Ops, SparseCore 0:
  13.8 62.0 all-reduce.5
  78.7 60.1 all-reduce.7
  141.8 29.4 reduce-scatter.3
  190.1 45.7 reduce-scatter.5
Sparse Core Ops, SparseCore 1:
  16.3 36.6 all-gather.2
  296.8 35.0 reduce-scatter.7
